TPU v7x, 32 devices: a whole 2x2x4 slice. The times are simulated.
32 devices in a mesh: elem: 8 (over z, x), cuts: 4 (over y, core).
Axes of the slice: x: 2, y: 2, z: 4, core: 2. Of those that a mesh axis runs over, the one named last changes fastest.
Arguments:
- basis: bfloat16 [8, 32768, 160], P('elem', 'cuts'), may hold values from -6 to 6
- quad_weight: float32 [8, 32768], P('elem', 'cuts'), may hold values from 0.5 to 2
- projectors: bfloat16 [8, 3, 20, 16, 32768], P('elem', None, None, None, 'cuts'), may hold values from -0.03125 to 0.03125
- species: int32 [8, 20], P('elem'), may hold values from 0 to 3
- counts: int32 [8, 20], P('elem'), may hold values from 1 to 16
- gamma_table: float32 [4, 16], replicated, may hold values from -0.4375 to 0.4375
Outputs:
- blocks: float32 [8, 3, 160, 160], P(None, None, 'elem', 'cuts')
Inputs may be any that keep to these rules, and one draw needn't show every extreme that they name: `counts`: each atom has at least one projector and at most 16.
All inputs are finite; a program needn't handle non-finite values.
Results may differ from a plain program's by a relative error of at most 0.004.
Values sent between devices are 32-bit elements; how exact they have to be, the bound alone decides.
No kernel may reach another device: no remote copies, remote signals or barrier semaphores. Data moves between devices by JAX's collectives and lax.ppermute only.
A program may use at most 64 MiB of HBM per device.

v0:
```python
import jax
import jax.numpy as jnp
from jax import lax
from jax.sharding import PartitionSpec as P


def passed_along(block, axis, distance):
    devices = range(lax.axis_size(axis))
    route = [((i - distance) % len(devices), i) for i in devices]
    return lax.ppermute(block, axis, route)


def pair_block(left, weights, right):
    return jnp.einsum("ib,ic->bc", left * weights[:, None], right, precision=lax.Precision.HIGHEST)


def local(basis, quad_weight, projectors, species, counts, gamma_table):
    width = basis.shape[2]
    groups, atoms, slots, points = projectors.shape[1:]
    span = atoms * slots
    quarter = width // lax.axis_size("cuts")
    cut_index = lax.axis_index("cuts")
    scaled = (basis[0].astype(jnp.float32) * quad_weight[0][:, None]).astype(jnp.bfloat16)
    partial_value = jnp.dot(
        projectors[0].reshape(groups * span, points), scaled, preferred_element_type=jnp.float32
    )
    onehot = (
        species[0][:, None] == jnp.arange(gamma_table.shape[0], dtype=jnp.int32)[None, :]
    ).astype(jnp.float32)
    table = jnp.dot(onehot, gamma_table, precision=lax.Precision.HIGHEST)
    active = (jnp.arange(slots, dtype=jnp.int32)[None, :] < counts[0][:, None]).astype(jnp.float32)
    energy = (table * active).reshape(span)
    full = lax.psum(partial_value, "cuts")
    left_whole, left_energy = passed_along((full[span:], energy), "elem", 1)
    right_whole, right_energy = passed_along((full[: 2 * span], energy), "elem", -1)
    start = cut_index * quarter
    own_share = lax.dynamic_slice_in_dim(full, start, quarter, 1)
    left_coef = lax.dynamic_slice_in_dim(left_whole, start, quarter, 1)
    right_coef = lax.dynamic_slice_in_dim(right_whole, start, quarter, 1)
    group0, group1, group2 = (full[:span], full[span : 2 * span], full[2 * span :])
    share0, share1, share2 = (own_share[:span], own_share[span : 2 * span], own_share[2 * span :])
    block_left = pair_block(group0, left_energy, left_coef[:span]) + pair_block(
        group1, energy, left_coef[span:]
    )
    block_diag = (
        pair_block(group0, left_energy, share0)
        + pair_block(group1, energy, share1)
        + pair_block(group2, right_energy, share2)
    )
    block_right = pair_block(group1, energy, right_coef[:span]) + pair_block(
        group2, right_energy, right_coef[span:]
    )
    stacked = jnp.stack([block_left, block_diag, block_right], axis=0)[None]
    return lax.all_to_all(stacked, "elem", split_axis=2, concat_axis=0, tiled=True)


def solution(mesh):
    in_specs = (
        P("elem", "cuts", None),
        P("elem", "cuts"),
        P("elem", None, None, None, "cuts"),
        P("elem", None),
        P("elem", None),
        P(),
    )
    out_specs = P(None, None, "elem", "cuts")
    return jax.shard_map(local, mesh=mesh, in_specs=in_specs, out_specs=out_specs, check_vma=False)
```

profile of v0, /device:TPU:0, one launch (start us, length us, event | category | flops | bytes accessed | tf_op | source)
XLA Modules:
  0.0 105.4 jit_solution(16012741648585391315)
XLA Ops:
  6.5 0.0 copy-start
  6.5 12.2 %fusion.4 = f32[960,160]{0,1:T(8,128)} fusion(bf16[960,8192]{1,0:T(8,128)(2,1)} %bitcast.32, bf16[1,8192,160]{1,2,0:T(8,128)(2,1)} %param.6, f32[8192]{0:T(1024)} %bitcast.33), kind=kOutput, calls=%fused_computation.4 | convolution fusion | flops 2520514560 | bytes 18997248 | tf_op jit(solution)/shard_map/dot_general | solution.py:24
  18.7 0.0 all-reduce.2.cloned.1.call-update
  18.8 0.2 convolution_select_fusion
  19.0 0.1 copy.18
  19.1 0.1 reshape.16
  19.1 2.9 %collective-permute-start = (f32[320]{0:T(512)S(1)}, f32[320]{0:T(512)S(1)}, u32[]{:S(2)}, u32[]{:S(2)}) collective-permute-start(f32[320]{0:T(512)S(1)} %reshape.16), channel_id=1, source_target_pairs={{28,0},{0,4},{4,8},{8,12},{12,16},{16,20},{20,24},{24,28},{29,1},{... | collective-permute-start | bytes 3848 | tf_op jit(solution)/shard_map/ppermute | solution.py:10
  22.1 3.1 %collective-permute-start.2 = (f32[320]{0:T(512)S(1)}, f32[320]{0:T(512)S(1)}, u32[]{:S(2)}, u32[]{:S(2)}) collective-permute-start(f32[320]{0:T(512)S(1)} %reshape.16), channel_id=1, source_target_pairs={{4,0},{8,4},{12,8},{16,12},{20,16},{24,20},{28,24},{0,28},{5,1},{9... | collective-permute-start | bytes 3848 | tf_op jit(solution)/shard_map/ppermute | solution.py:10
  25.2 30.2 %all-reduce.2.cloned.1.call-done = f32[960,160]{0,1:T(8,128)} async-done(((f32[960,160]{0,1:T(8,128)}), f32[960,160]{0,1:T(8,128)}) %all-reduce.2.cloned.1.call-update) | async-done | bytes 614416 | tf_op jit(solution)/shard_map/psum | solution.py:33
  55.4 1.4 %fusion.33 = (f32[640,160]{0,1:T(8,128)S(1)}, f32[640,160]{0,1:T(8,128)S(1)}) fusion(f32[960,160]{0,1:T(8,128)} %all-reduce.2.cloned.1.call-done), kind=kLoop, calls=%fused_computation.42 | loop fusion | bytes 1638400 | tf_op jit(solution)/shard_map/slice | solution.py:34
  56.8 1.5 %collective-permute-start.1 = (f32[640,160]{0,1:T(8,128)S(1)}, f32[640,160]{0,1:T(8,128)S(1)}, u32[]{:S(2)}, u32[]{:S(2)}) collective-permute-start(f32[640,160]{0,1:T(8,128)S(1)} %get-tuple-element.5), channel_id=1, source_target_pairs={{28,0},{0,4},{4,8},{8,12},{12,16},{16,20},{20,24},{24,28},{29,1},{... | collective-permute-start | bytes 1228808 | tf_op jit(solution)/shard_map/ppermute | solution.py:10
  58.3 3.3 %collective-permute-start.3 = (f32[640,160]{0,1:T(8,128)S(1)}, f32[640,160]{0,1:T(8,128)S(1)}, u32[]{:S(2)}, u32[]{:S(2)}) collective-permute-start(f32[640,160]{0,1:T(8,128)S(1)} %get-tuple-element.6), channel_id=1, source_target_pairs={{4,0},{8,4},{12,8},{16,12},{20,16},{24,20},{28,24},{0,28},{5,1},{9... | collective-permute-start | bytes 1228808 | tf_op jit(solution)/shard_map/ppermute | solution.py:10
  61.5 1.5 %fusion.13 = f32[160,40]{0,1:T(8,128)S(1)} fusion(f32[960,160]{0,1:T(8,128)} %all-reduce.2.cloned.1.call-done, f32[320]{0:T(512)S(1)} %reshape.16, s32[]{:T(128)S(6)} %add.24, s32[]{:T(128)S(6)} %select_n.2), kind=kOutput, calls=%fused_computation.19 | convolution fusion | flops 24627200 | bytes 334088 | tf_op jit(solution)/shard_map/ib,ic->bc/dot_general | solution.py:14
  63.0 0.0 collective-permute-done.2
  63.0 1.4 %fusion.12 = f32[160,40]{0,1:T(8,128)S(1)} fusion(f32[960,160]{0,1:T(8,128)} %all-reduce.2.cloned.1.call-done, f32[320]{0:T(512)S(1)} %collective-permute-done.2, s32[]{:T(128)S(6)} %add.26, s32[]{:T(128)S(6)} %select_n.2), kind=kOutput, calls=%fused_computation.18 | convolution fusion | flops 24627200 | bytes 334088 | tf_op jit(solution)/shard_map/ib,ic->bc/dot_general | solution.py:14
  64.4 0.0 collective-permute-done
  64.4 1.4 %fusion.10 = f32[1,160,40]{1,2,0:T(8,128)S(1)} fusion(f32[160,40]{0,1:T(8,128)S(1)} %fusion.12, f32[160,40]{0,1:T(8,128)S(1)} %fusion.13, f32[960,160]{0,1:T(8,128)} %all-reduce.2.cloned.1.call-done, f32[320]{0:T(512)S(1)} %collective-permute-done, s32[]{:T(128)S(6)} %select_n.2), kind=kOutput, calls=%fused_computation.11 | convolution fusion | flops 24640000 | bytes 385284 | tf_op jit(solution)/shard_map/ib,ic->bc/dot_general | solution.py:14
  65.8 9.1 %collective-permute-done.1 = f32[640,160]{0,1:T(8,128)S(1)} collective-permute-done((f32[640,160]{0,1:T(8,128)S(1)}, f32[640,160]{0,1:T(8,128)S(1)}, u32[]{:S(2)}, u32[]{:S(2)}) %collective-permute-start.1) | collective-permute-done | bytes 409632 | tf_op jit(solution)/shard_map/ppermute | solution.py:10
  74.9 1.5 %fusion.14 = f32[160,40]{0,1:T(8,128)S(1)} fusion(f32[960,160]{0,1:T(8,128)} %all-reduce.2.cloned.1.call-done, f32[320]{0:T(512)S(1)} %reshape.16, f32[640,160]{0,1:T(8,128)S(1)} %collective-permute-done.1, s32[]{:T(128)S(6)} %add.24, s32[]{:T(128)S(6)} %select_n.2), kind=kOutput, calls=%fused_computation.20 | convolution fusion | flops 24627200 | bytes 334856 | tf_op jit(solution)/shard_map/ib,ic->bc/dot_general | solution.py:14
  76.3 1.4 %fusion.8 = f32[1,160,40]{1,2,0:T(8,128)S(1)} fusion(f32[160,40]{0,1:T(8,128)S(1)} %fusion.14, f32[960,160]{0,1:T(8,128)} %all-reduce.2.cloned.1.call-done, f32[320]{0:T(512)S(1)} %collective-permute-done, f32[640,160]{0,1:T(8,128)S(1)} %collective-permute-done.1, s32[]{:T(128)S(6)} %select_n.2), kind=kOutput, calls=%fused_computation.9 | convolution fusion | flops 24633600 | bytes 375812 | tf_op jit(solution)/shard_map/ib,ic->bc/dot_general | solution.py:14
  77.7 0.0 collective-permute-done.3
  77.7 1.4 %fusion.11 = f32[160,40]{0,1:T(8,128)S(1)} fusion(f32[960,160]{0,1:T(8,128)} %all-reduce.2.cloned.1.call-done, f32[320]{0:T(512)S(1)} %collective-permute-done.2, f32[640,160]{0,1:T(8,128)S(1)} %collective-permute-done.3, s32[]{:T(128)S(6)} %add.24, s32[]{:T(128)S(6)} %select_n.2), kind=kOutput, calls=%fused_computation.17 | convolution fusion | flops 24627200 | bytes 334856 | tf_op jit(solution)/shard_map/ib,ic->bc/dot_general | solution.py:14
  79.1 1.5 %fusion.7 = f32[1,160,40]{1,2,0:T(8,128)S(1)} fusion(f32[160,40]{0,1:T(8,128)S(1)} %fusion.11, f32[960,160]{0,1:T(8,128)} %all-reduce.2.cloned.1.call-done, f32[320]{0:T(512)S(1)} %reshape.16, f32[640,160]{0,1:T(8,128)S(1)} %collective-permute-done.3, s32[]{:T(128)S(6)} %select_n.2), kind=kOutput, calls=%fused_computation.6 | convolution fusion | flops 24633600 | bytes 375812 | tf_op jit(solution)/shard_map/ib,ic->bc/dot_general | solution.py:14
  80.6 0.2 copy.19
  80.8 0.5 broadcast.11
  81.3 1.4 %reduce = f32[160,3,40]{2,1,0:T(4,128)S(1)} reduce(f32[160,3,1,40]{3,2,1,0:T(1,128)S(1)} %bitcast.31, f32[]{:T(128)} %broadcast.11), dimensions={2}, to_apply=%bitcast.24.reduce_sub_computation | reduce | bytes 153604
  82.8 0.3 reshape.17
  83.1 13.3 %all_to_all.18 = f32[8,1,2400]{2,1,0:T(1,128)S(1)} all-to-all(f32[8,1,2400]{2,1,0:T(1,128)S(1)} %reshape.17), channel_id=1, replica_groups=mesh['elem'=8,'cuts'=4] {'elem'}, dimensions={0} | all-to-all | bytes 153600 | tf_op jit(solution)/shard_map/all_to_all | solution.py:54
  96.4 0.8 reduce.1
  97.2 0.5 reshape.18
  97.7 0.2 copy.20
  97.9 0.7 copy.23
  (7 shorter events, 0.0 us)
Async XLA Ops:
  6.5 12.2 %copy-start = (f32[4,16]{1,0:T(4,128)S(1)}, f32[4,16]{1,0:T(4,128)}, u32[]{:S(2)}) copy-start(f32[4,16]{1,0:T(4,128)} %param.11) | copy-start | bytes 772
  6.5 48.9 %all-reduce.2.cloned.1.call-start = ((), (), s32[]{:S(2)}) async-start(), calls=%async_computation.1 | async-start | bytes 1310720 | tf_op jit(solution)/shard_map/psum | solution.py:33
  6.5 12.2 %copy-start.1 = (s32[1,20]{1,0:T(1,128)S(1)}, s32[1,20]{1,0:T(1,128)}, u32[]{:S(2)}) copy-start(s32[1,20]{1,0:T(1,128)} %param.9) | copy-start | bytes 244
  6.5 12.2 %copy-start.2 = (s32[1,20]{1,0:T(1,128)S(1)}, s32[1,20]{1,0:T(1,128)}, u32[]{:S(2)}) copy-start(s32[1,20]{1,0:T(1,128)} %param.10) | copy-start | bytes 244
  19.1 45.3 %collective-permute-start = (f32[320]{0:T(512)S(1)}, f32[320]{0:T(512)S(1)}, u32[]{:S(2)}, u32[]{:S(2)}) collective-permute-start(f32[320]{0:T(512)S(1)} %reshape.16), channel_id=1, source_target_pairs={{28,0},{0,4},{4,8},{8,12},{12,16},{16,20},{20,24},{24,28},{29,1},{... | collective-permute-start | bytes 3848 | tf_op jit(solution)/shard_map/ppermute | solution.py:10
  22.1 40.9 %collective-permute-start.2 = (f32[320]{0:T(512)S(1)}, f32[320]{0:T(512)S(1)}, u32[]{:S(2)}, u32[]{:S(2)}) collective-permute-start(f32[320]{0:T(512)S(1)} %reshape.16), channel_id=1, source_target_pairs={{4,0},{8,4},{12,8},{16,12},{20,16},{24,20},{28,24},{0,28},{5,1},{9... | collective-permute-start | bytes 3848 | tf_op jit(solution)/shard_map/ppermute | solution.py:10
  56.8 18.1 %collective-permute-start.1 = (f32[640,160]{0,1:T(8,128)S(1)}, f32[640,160]{0,1:T(8,128)S(1)}, u32[]{:S(2)}, u32[]{:S(2)}) collective-permute-start(f32[640,160]{0,1:T(8,128)S(1)} %get-tuple-element.5), channel_id=1, source_target_pairs={{28,0},{0,4},{4,8},{8,12},{12,16},{16,20},{20,24},{24,28},{29,1},{... | collective-permute-start | bytes 1228808 | tf_op jit(solution)/shard_map/ppermute | solution.py:10
  58.3 19.4 %collective-permute-start.3 = (f32[640,160]{0,1:T(8,128)S(1)}, f32[640,160]{0,1:T(8,128)S(1)}, u32[]{:S(2)}, u32[]{:S(2)}) collective-permute-start(f32[640,160]{0,1:T(8,128)S(1)} %get-tuple-element.6), channel_id=1, source_target_pairs={{4,0},{8,4},{12,8},{16,12},{20,16},{24,20},{28,24},{0,28},{5,1},{9... | collective-permute-start | bytes 1228808 | tf_op jit(solution)/shard_map/ppermute | solution.py:10
Sparse Core Ops, SparseCore 0:
  18.9 36.5 all-reduce.1
where the time goes:
time: 106 us; the launch traced here: 105 us
  waiting for transfers between devices  39.3 us (37%)
  matrix products  22.3 us (21%)
  between operations  13.5 us (13%)
  blocking collectives  13.3 us (13%)
  starting transfers between devices  10.8 us (10%)
  local copies, waits for them, and re-layouts  3.83 us (4%)
  other arithmetic  2.29 us (2%)
    psum x1, waiting for transfers between devices, local(): full = lax.psum(partial_value, 'cuts')  30.2 us
    all_to_all x1, blocking collectives, local(): lax.all_to_all(stacked, 'elem', split_axis=2, concat_axis=0, tiled=True)  13.3 us
    dot_general x1, matrix products, local(): jnp.dot(projectors[0].reshape(groups * span, points), scaled, preferred_e...  12.2 us
    ppermute x4, starting transfers between devices, passed_along(): return lax.ppermute(block, axis, route)  10.8 us
    dot_general x7, matrix products, pair_block(): jnp.einsum('ib,ic->bc', left * weights[:, None], right, precision=lax.Pre...  9.95 us
    ppermute x4, waiting for transfers between devices, passed_along(): return lax.ppermute(block, axis, route)  9.06 us
  transfers between devices with their start and end apart: 5, of which 2 were waited for; matrix products, arithmetic and copies ran while one was open for 8% of the time, Pallas kernels for 0%

commit v1 on v0

--- a/solution.py
+++ b/solution.py
@@ -30,7 +30,7 @@
     table = jnp.dot(onehot, gamma_table, precision=lax.Precision.HIGHEST)
     active = (jnp.arange(slots, dtype=jnp.int32)[None, :] < counts[0][:, None]).astype(jnp.float32)
     energy = (table * active).reshape(span)
-    full = lax.psum(partial_value, "cuts")
+    full = jnp.sum(lax.all_gather(partial_value, "cuts"), axis=0)
     left_whole, left_energy = passed_along((full[span:], energy), "elem", 1)
     right_whole, right_energy = passed_along((full[: 2 * span], energy), "elem", -1)
     start = cut_index * quarter

time: 106 us -> 95 us (0.90)
  matrix products: 22.3 us -> 15.6 us
  waiting for transfers between devices: 39.3 us -> 36.8 us
  other arithmetic: 2.29 us -> 4.34 us
  blocking collectives: 13.3 us -> 11.6 us
  local copies, waits for them, and re-layouts: 3.83 us -> 2.65 us
    psum x1 -> x0, waiting for transfers between devices: 30.2 us -> none  [local(): full = lax.psum(partial_value, 'cuts')]
    all_gather x0 -> x1, waiting for transfers between devices: none -> 22 us  [local(): full = jnp.sum(lax.all_gather(partial_value, 'cuts'), axis=0)]
    dot_general x7, matrix products: 9.95 us -> 3.21 us  [pair_block(): jnp.einsum('ib,ic->bc', left * weights[:, None], right, precision=lax.Pre...]
    ppermute x4, waiting for transfers between devices: 9.06 us -> 14.8 us  [passed_along(): return lax.ppermute(block, axis, route)]
    reduce_sum x0 -> x1, other arithmetic: none -> 2.05 us  [local(): full = jnp.sum(lax.all_gather(partial_value, 'cuts'), axis=0)]
    all_to_all x1, blocking collectives: 13.3 us -> 11.6 us  [local(): lax.all_to_all(stacked, 'elem', split_axis=2, concat_axis=0, tiled=True)]
    slice x1, local copies, waits for them, and re-layouts: 1.35 us -> 0.17 us  [local(): left_whole, left_energy = passed_along((full[span:], energy), 'elem', 1)]
  transfers between devices with their start and end apart: 5 -> 5, of which waited for: 2 -> 2; matrix products, arithmetic and copies ran while one was open for 8% -> 5% of each run, Pallas kernels for 0% -> 0%
where the time goes in v1:
time: 95 us; the launch traced here: 94.8 us
  waiting for transfers between devices  36.8 us (39%)
  matrix products  15.6 us (16%)
  between operations  13.5 us (14%)
  blocking collectives  11.6 us (12%)
  starting transfers between devices  10.3 us (11%)
  other arithmetic  4.34 us (5%)
  local copies, waits for them, and re-layouts  2.65 us (3%)
    all_gather x1, waiting for transfers between devices, local(): full = jnp.sum(lax.all_gather(partial_value, 'cuts'), axis=0)  22 us
    ppermute x4, waiting for transfers between devices, passed_along(): return lax.ppermute(block, axis, route)  14.8 us
    dot_general x1, matrix products, local(): jnp.dot(projectors[0].reshape(groups * span, points), scaled, preferred_e...  12.2 us
    all_to_all x1, blocking collectives, local(): lax.all_to_all(stacked, 'elem', split_axis=2, concat_axis=0, tiled=True)  11.6 us
    ppermute x4, starting transfers between devices, passed_along(): return lax.ppermute(block, axis, route)  10.3 us
    dot_general x7, matrix products, pair_block(): jnp.einsum('ib,ic->bc', left * weights[:, None], right, precision=lax.Pre...  3.21 us
    reduce_sum x1, other arithmetic, local(): full = jnp.sum(lax.all_gather(partial_value, 'cuts'), axis=0)  2.05 us
  transfers between devices with their start and end apart: 5, of which 2 were waited for; matrix products, arithmetic and copies ran while one was open for 5% of the time, Pallas kernels for 0%

profile of v1, /device:TPU:0, one launch (start us, length us, event | category | flops | bytes accessed | tf_op | source)
XLA Modules:
  0.0 94.8 jit_solution(16200541368524280856)
XLA Ops:
  6.5 12.2 %fusion.4 = f32[1,960,160]{1,2,0:T(8,128)} fusion(bf16[960,8192]{1,0:T(8,128)(2,1)} %bitcast.34, bf16[1,8192,160]{1,2,0:T(8,128)(2,1)} %param.6, f32[8192]{0:T(1024)} %bitcast.35), kind=kOutput, calls=%fused_computation.4 | convolution fusion | flops 2520514560 | bytes 18997248 | tf_op jit(solution)/shard_map/dot_general | solution.py:24
  18.7 0.0 all-gather.4.cloned.1.call-update
  18.8 0.2 convolution_select_fusion
  19.0 0.1 copy.18
  19.1 0.1 reshape.16
  19.1 6.0 %collective-permute-start.2 = (f32[320]{0:T(512)S(1)}, f32[320]{0:T(512)S(1)}, u32[]{:S(2)}, u32[]{:S(2)}) collective-permute-start(f32[320]{0:T(512)S(1)} %reshape.16), channel_id=1, source_target_pairs={{4,0},{8,4},{12,8},{16,12},{20,16},{24,20},{28,24},{0,28},{5,1},{9... | collective-permute-start | bytes 3848 | tf_op jit(solution)/shard_map/ppermute | solution.py:10
  25.1 0.0 collective-permute-start
  25.1 22.0 %all-gather.4.cloned.1.call-done = f32[4,960,160]{1,2,0:T(8,128)} async-done(((f32[1,960,160]{1,2,0:T(8,128)}), f32[4,960,160]{1,2,0:T(8,128)}) %all-gather.4.cloned.1.call-update) | async-done | bytes 2457616 | tf_op jit(solution)/shard_map/all_gather | solution.py:33
  47.2 2.1 %reduce_sum.9 = f32[960,160]{0,1:T(8,128)S(1)} reduce(f32[4,960,160]{1,2,0:T(8,128)} %all-gather.4.cloned.1.call-done, f32[]{:T(128)} %constant.5.clone.1), dimensions={0}, to_apply=%region_0.0 | reduce | flops 460800 | bytes 3072004 | tf_op jit(solution)/shard_map/reduce_sum | solution.py:33
  49.2 0.2 fusion.33
  49.4 4.3 %collective-permute-start.3 = (f32[640,160]{0,1:T(8,128)S(1)}, f32[640,160]{0,1:T(8,128)S(1)}, u32[]{:S(2)}, u32[]{:S(2)}) collective-permute-start(f32[640,160]{0,1:T(8,128)S(1)} %get-tuple-element.6), channel_id=1, source_target_pairs={{4,0},{8,4},{12,8},{16,12},{20,16},{24,20},{28,24},{0,28},{5,1},{9... | collective-permute-start | bytes 1228808 | tf_op jit(solution)/shard_map/ppermute | solution.py:10
  53.7 0.0 collective-permute-start.1
  53.7 0.5 fusion.13
  54.2 0.0 collective-permute-done.2
  54.2 0.4 fusion.12
  54.6 0.0 collective-permute-done
  54.6 0.4 fusion.10
  55.1 14.8 %collective-permute-done.3 = f32[640,160]{0,1:T(8,128)S(1)} collective-permute-done((f32[640,160]{0,1:T(8,128)S(1)}, f32[640,160]{0,1:T(8,128)S(1)}, u32[]{:S(2)}, u32[]{:S(2)}) %collective-permute-start.3) | collective-permute-done | bytes 409632 | tf_op jit(solution)/shard_map/ppermute | solution.py:10
  69.8 0.5 fusion.11
  70.3 0.5 fusion.7
  70.8 0.0 collective-permute-done.1
  70.8 0.5 fusion.14
  71.3 0.4 fusion.8
  71.8 0.2 copy.19
  71.9 0.5 broadcast.11
  72.4 1.4 %reduce.1 = f32[160,3,40]{2,1,0:T(4,128)S(1)} reduce(f32[160,3,1,40]{3,2,1,0:T(1,128)S(1)} %bitcast.33, f32[]{:T(128)} %broadcast.11), dimensions={2}, to_apply=%bitcast.26.reduce_sub_computation | reduce | bytes 153604
  73.9 0.3 reshape.21
  74.2 11.6 %all_to_all.18 = f32[8,1,2400]{2,1,0:T(1,128)S(1)} all-to-all(f32[8,1,2400]{2,1,0:T(1,128)S(1)} %reshape.21), channel_id=1, replica_groups=mesh['elem'=8,'cuts'=4] {'elem'}, dimensions={0} | all-to-all | bytes 153600 | tf_op jit(solution)/shard_map/all_to_all | solution.py:54
  85.8 0.8 reduce.2
  86.6 0.5 reshape.22
  87.1 0.2 copy.20
  87.2 0.7 copy.23
  (8 shorter events, 0.0 us)
Async XLA Ops:
  6.5 12.2 %copy-start = (f32[4,16]{1,0:T(4,128)S(1)}, f32[4,16]{1,0:T(4,128)}, u32[]{:S(2)}) copy-start(f32[4,16]{1,0:T(4,128)} %param.11) | copy-start | bytes 772
  6.5 40.6 %all-gather.4.cloned.1.call-start = ((), (), s32[]{:S(2)}) async-start(), calls=%async_computation.1 | async-start | bytes 3276800 | tf_op jit(solution)/shard_map/all_gather | solution.py:33
  6.5 12.2 %copy-start.1 = (s32[1,20]{1,0:T(1,128)S(1)}, s32[1,20]{1,0:T(1,128)}, u32[]{:S(2)}) copy-start(s32[1,20]{1,0:T(1,128)} %param.9) | copy-start | bytes 244
  6.5 12.2 %copy-start.2 = (s32[1,20]{1,0:T(1,128)S(1)}, s32[1,20]{1,0:T(1,128)}, u32[]{:S(2)}) copy-start(s32[1,20]{1,0:T(1,128)} %param.10) | copy-start | bytes 244
  19.1 35.0 %collective-permute-start.2 = (f32[320]{0:T(512)S(1)}, f32[320]{0:T(512)S(1)}, u32[]{:S(2)}, u32[]{:S(2)}) collective-permute-start(f32[320]{0:T(512)S(1)} %reshape.16), channel_id=1, source_target_pairs={{4,0},{8,4},{12,8},{16,12},{20,16},{24,20},{28,24},{0,28},{5,1},{9... | collective-permute-start | bytes 3848 | tf_op jit(solution)/shard_map/ppermute | solution.py:10
  25.1 29.5 %collective-permute-start = (f32[320]{0:T(512)S(1)}, f32[320]{0:T(512)S(1)}, u32[]{:S(2)}, u32[]{:S(2)}) collective-permute-start(f32[320]{0:T(512)S(1)} %reshape.16), channel_id=1, source_target_pairs={{28,0},{0,4},{4,8},{8,12},{12,16},{16,20},{20,24},{24,28},{29,1},{... | collective-permute-start | bytes 3848 | tf_op jit(solution)/shard_map/ppermute | solution.py:10
  49.4 20.4 %collective-permute-start.3 = (f32[640,160]{0,1:T(8,128)S(1)}, f32[640,160]{0,1:T(8,128)S(1)}, u32[]{:S(2)}, u32[]{:S(2)}) collective-permute-start(f32[640,160]{0,1:T(8,128)S(1)} %get-tuple-element.6), channel_id=1, source_target_pairs={{4,0},{8,4},{12,8},{16,12},{20,16},{24,20},{28,24},{0,28},{5,1},{9... | collective-permute-start | bytes 1228808 | tf_op jit(solution)/shard_map/ppermute | solution.py:10
  53.7 17.1 %collective-permute-start.1 = (f32[640,160]{0,1:T(8,128)S(1)}, f32[640,160]{0,1:T(8,128)S(1)}, u32[]{:S(2)}, u32[]{:S(2)}) collective-permute-start(f32[640,160]{0,1:T(8,128)S(1)} %get-tuple-element.5), channel_id=1, source_target_pairs={{28,0},{0,4},{4,8},{8,12},{12,16},{16,20},{20,24},{24,28},{29,1},{... | collective-permute-start | bytes 1228808 | tf_op jit(solution)/shard_map/ppermute | solution.py:10
Sparse Core Ops, SparseCore 0:
  18.9 28.2 all-gather.3
